TPU v7x, 256 devices: a whole 4x4x8 slice. The times are simulated.
256 devices in a mesh: seq: 16 (over x, y), exp: 16 (over z, core).
Axes of the slice: x: 4, y: 4, z: 8, core: 2. Of those that a mesh axis runs over, the one named last changes fastest.
Arguments:
- mixer_input: bfloat16 [16384, 4096], P('seq', 'exp'), may hold values from -6 to 6
- gate_input: bfloat16 [16384, 4096], P('seq', 'exp'), may hold values from -6 to 6
- write_keys: bfloat16 [16384, 128], P('seq'), may hold values from -6 to 6
- read_queries: bfloat16 [16384, 128], P('seq'), may hold values from -0.5 to 0.5
- step_size: float32 [64, 16384], P('exp', 'seq'), may hold values from 0 to 1, as said below
- log_decay: float32 [64, 16384], P('exp', 'seq'), may hold values from -1 to 0, as said below
- skip_gain: float32 [64], P('exp'), may hold values from 0.5 to 1.5
- out_weight: bfloat16 [4096, 2048], P('exp'), may hold values from -0.09375 to 0.09375
- residual: bfloat16 [16384, 2048], P(('seq', 'exp')), may hold values from -6 to 6
- norm_gain: float32 [2048], replicated, may hold values from 0.25 to 1.75
- routes: int32 [16384, 6], P(('seq', 'exp')), may hold values from 0 to 63, all different within a row; in each aligned block of 64 rows (0 to 63, 64 to 127, ...) at most 8 rows name the same one
- route_weight: float32 [16384, 6], P(('seq', 'exp')), may hold values from 0.1 to 0.5
- expert_gate: bfloat16 [256, 352, 2048], P(('seq', 'exp')), may hold values from -0.125 to 0.125
- expert_up: bfloat16 [256, 352, 2048], P(('seq', 'exp')), may hold values from -0.125 to 0.125
- expert_down: bfloat16 [256, 352, 2048], P(('seq', 'exp')), may hold values from -0.15625 to 0.15625
Outputs:
- block_output: bfloat16 [16384, 2048], P(('seq', 'exp'))
Inputs may be any that keep to these rules, and one draw needn't show every extreme that they name: `routes`: each row names 6 different experts; in each aligned block of 64 rows (the rows of one device) no expert is named by more than 8 rows, a bound that some block reaches. `step_size`: positive. `log_decay`: not positive.
All inputs are finite; a program needn't handle non-finite values.
Results may differ from a plain program's by a relative error of at most 0.015.
Values may be sent and summed in bfloat16 or wider, within the bound.
No kernel may reach another device: no remote copies, remote signals or barrier semaphores. Data moves between devices by JAX's collectives and lax.ppermute only.
A program may use at most 128 MiB of HBM per device.

v0:
```python
import jax
import jax.numpy as jnp
from jax import lax
from jax.sharding import PartitionSpec as P

HEAD_DIM = 64
STATE = 128
TOP = 6
SPLIT = 4
STRETCH = 256


def prefix(shard, axis, join, neutral):
    place = lax.axis_index(axis)
    gathered = jax.tree.map(
        lambda a, kind: lax.all_gather(a.astype(kind), axis), shard, (jnp.bfloat16, jnp.bfloat16)
    )
    state = jax.tree.map(lambda a, e: jnp.zeros_like(a) + jnp.asarray(e, a.dtype), shard, neutral)

    def one(turn, state):
        return join(
            state,
            jax.tree.map(
                lambda a, own: lax.dynamic_index_in_dim(a, turn, 0, False).astype(own.dtype),
                gathered,
                shard,
            ),
        )

    return lax.fori_loop(0, place, one, state)


def join_states(earlier, later_part):
    return (
        earlier[0] + later_part[0],
        jnp.exp(later_part[0])[:, None, None] * earlier[1] + later_part[1],
    )


def shards(
    mixer_input,
    gate_input,
    write_keys,
    read_queries,
    step_size,
    log_decay,
    skip_gain,
    out_weight,
    residual,
    norm_gain,
    routes,
    route_weight,
    expert_gate,
    expert_up,
    expert_down,
):
    length = mixer_input.shape[0]
    head_count = step_size.shape[0]
    blocks = length // STRETCH
    inputs = mixer_input.reshape(blocks, STRETCH, head_count, HEAD_DIM)
    key_rows = write_keys.reshape(blocks, STRETCH, STATE)
    queries = read_queries.reshape(blocks, STRETCH, STATE)
    step_rows = step_size.reshape(head_count, blocks, STRETCH).transpose(1, 0, 2)
    cumulative = jnp.cumsum(log_decay.reshape(head_count, blocks, STRETCH), axis=2).transpose(
        1, 0, 2
    )
    location_values = jnp.arange(STRETCH, dtype=jnp.int32)
    causal = location_values[:, None] >= location_values[None, :]
    scores = jnp.einsum("cin,cjn->cij", queries, key_rows, preferred_element_type=jnp.float32)
    spread = cumulative[:, :, :, None] - cumulative[:, :, None, :]
    decays = jnp.where(causal, jnp.exp(jnp.where(causal, spread, 0.0)), 0.0)
    mixing = (scores[:, None] * decays * step_rows[:, :, None, :]).astype(jnp.bfloat16)
    local_out = jnp.einsum("chij,cjhp->cihp", mixing, inputs, preferred_element_type=jnp.float32)
    tail_scale = jnp.exp(cumulative[:, :, -1:] - cumulative) * step_rows
    weighted = (inputs.astype(jnp.float32) * tail_scale.transpose(0, 2, 1)[..., None]).astype(
        jnp.bfloat16
    )
    block_state = jnp.einsum(
        "cjhp,cjn->chpn", weighted, key_rows, preferred_element_type=jnp.float32
    )
    totals = cumulative[:, :, -1]

    def advance(carry_state, pieces):
        block_total, fresh_state = pieces
        return (jnp.exp(block_total)[:, None, None] * carry_state + fresh_state, carry_state)

    zero_state = jnp.zeros((head_count, HEAD_DIM, STATE), jnp.float32)
    end_local, entering_local = lax.scan(advance, zero_state, (totals, block_state))
    device_decay = jnp.sum(totals, axis=0)
    before = prefix(
        (device_decay, end_local), "seq", join_states, (jnp.zeros_like(device_decay), zero_state)
    )
    before_state = before[1]
    before_blocks = jnp.cumsum(totals, axis=0) - totals
    entering = jnp.exp(before_blocks)[:, :, None, None] * before_state[None] + entering_local
    carried = jnp.einsum(
        "cin,chpn->cihp", queries.astype(jnp.float32), entering, precision=lax.Precision.HIGHEST
    )
    carried = carried * jnp.exp(cumulative).transpose(0, 2, 1)[..., None]
    result = local_out + carried + skip_gain[None, None, :, None] * inputs.astype(jnp.float32)
    gated_out = (
        result.reshape(length, head_count * HEAD_DIM) * jax.nn.silu(gate_input.astype(jnp.float32))
    ).astype(jnp.bfloat16)
    row_count = residual.shape[0]
    mixer_out = lax.psum_scatter(
        jnp.dot(gated_out, out_weight, preferred_element_type=jnp.float32).astype(jnp.bfloat16),
        "exp",
        scatter_dimension=0,
        tiled=True,
    ).astype(jnp.float32)
    stream = (residual.astype(jnp.float32) + mixer_out).astype(jnp.bfloat16)
    widened = stream.astype(jnp.float32)
    normed = (
        widened * lax.rsqrt(jnp.mean(widened * widened, axis=-1, keepdims=True) + 1e-06) * norm_gain
    ).astype(jnp.bfloat16)
    seq_count = lax.axis_size("seq")
    exp_count = lax.axis_size("exp")
    row_experts = exp_count // SPLIT
    experts = seq_count * row_experts
    capacity = min(row_count, max(2, (4 * TOP * row_count + 3 * experts - 1) // (3 * experts)))
    flat_routes = routes.reshape(-1)
    onehot = (flat_routes[:, None] == jnp.arange(experts, dtype=jnp.int32)[None, :]).astype(
        jnp.int32
    )
    earlier_count = jnp.cumsum(onehot, axis=0) - onehot
    slot_index = jnp.sum(earlier_count * onehot, axis=1)
    target = (
        flat_routes % row_experts * (seq_count * capacity)
        + flat_routes // row_experts * capacity
        + slot_index
    )
    owner_row = jnp.arange(flat_routes.shape[0], dtype=jnp.int32) // TOP
    source = jnp.zeros((experts * capacity,), jnp.int32).at[target].set(owner_row)
    filled = jnp.zeros((experts * capacity,), jnp.bool_).at[target].set(True)
    outgoing = jnp.where(filled[:, None], normed[source], jnp.zeros((), jnp.bfloat16))
    outgoing = outgoing.reshape(row_experts, seq_count, capacity, -1)
    arrived = lax.all_to_all(outgoing, "seq", split_axis=1, concat_axis=1, tiled=True)
    copies = jnp.repeat(arrived, SPLIT, axis=0)
    block = lax.all_to_all(copies, "exp", split_axis=0, concat_axis=0, tiled=True)
    flat_rows = block.reshape(-1, block.shape[-1])
    contract = (((1,), (1,)), ((), ()))
    gate_val = lax.dot_general(
        flat_rows, expert_gate[0], contract, preferred_element_type=jnp.float32
    )
    up_val = lax.dot_general(flat_rows, expert_up[0], contract, preferred_element_type=jnp.float32)
    activated = (jax.nn.silu(gate_val) * up_val).astype(jnp.bfloat16)
    piece_out = jnp.dot(activated, expert_down[0], preferred_element_type=jnp.float32).astype(
        jnp.bfloat16
    )
    piece_out = piece_out.reshape(block.shape)
    returned = lax.all_to_all(
        lax.all_to_all(piece_out, "seq", split_axis=1, concat_axis=1, tiled=True),
        "exp",
        split_axis=0,
        concat_axis=0,
        tiled=True,
    )
    summed = jnp.sum(
        returned.reshape(row_experts, SPLIT, seq_count, capacity, -1).astype(jnp.float32), axis=1
    )
    results = summed.reshape(experts * capacity, -1)[target]
    expert_sum = jnp.sum(
        (results * route_weight.reshape(-1)[:, None]).reshape(row_count, TOP, -1), axis=1
    )
    return (stream.astype(jnp.float32) + expert_sum).astype(jnp.bfloat16)


def solution(mesh):
    return jax.shard_map(
        shards,
        mesh=mesh,
        in_specs=(
            P("seq", "exp"),
            P("seq", "exp"),
            P("seq", None),
            P("seq", None),
            P("exp", "seq"),
            P("exp", "seq"),
            P("exp"),
            P("exp", None),
            P(("seq", "exp"), None),
            P(),
            P(("seq", "exp"), None),
            P(("seq", "exp"), None),
            P(("seq", "exp"), None, None),
            P(("seq", "exp"), None, None),
            P(("seq", "exp"), None, None),
        ),
        out_specs=P(("seq", "exp"), None),
        check_vma=False,
    )
```

profile of v0, /device:TPU:1, one launch (start us, length us, event | category | flops | bytes accessed | tf_op | source)
XLA Modules:
  0.0 738.1 jit_solution(7842727586102235308)
XLA Ops:
  6.5 0.9 reshape.254
  7.4 4.8 reduce-window.14
  12.3 0.1 copy.65
  12.5 0.1 copy.66
  12.6 0.1 broadcast_add_fusion
  12.7 0.3 copy.67
  13.0 0.8 copy-done.6
  13.8 2.0 reshape.309
  15.8 0.5 copy.72
  16.5 1.3 fusion.29
  17.8 3.1 while.26
  17.8 0.7 bitcast_dynamic-update-slice_fusion.2
  18.6 0.7 bitcast_dynamic-update-slice_fusion.2
  19.4 0.7 bitcast_dynamic-update-slice_fusion.2
  20.2 0.7 bitcast_dynamic-update-slice_fusion.2
  20.8 0.1 bitcast_add_fusion.2
  20.9 0.6 convert_element_type.96
  21.7 0.6 dynamic-slice
  23.0 0.2 dynamic-update-slice
  23.2 34.3 %all-reduce = bf16[64]{0:T(256)(128)(2,1)S(1)} all-reduce(bf16[64]{0:T(256)(128)(2,1)S(1)} %dynamic-update-slice), channel_id=2, replica_groups=mesh['seq'=16,'exp'=16] {'seq'}, use_global_device_ids=true, to_apply=%add | all-reduce | flops 64 | bytes 256
  57.5 0.1 reshape.299
  57.6 2.1 copy.77
  59.7 0.7 subtract_exponential_fusion
  60.4 0.3 fusion.58
  60.7 1.4 fusion.14
  62.1 9.7 %all-gather.4.cloned.1.call-done = bf16[64,64,128]{2,1,0:T(8,128)(2,1)} async-done(((bf16[4,64,128]{2,1,0:T(8,128)(2,1)}), bf16[64,64,128]{2,1,0:T(8,128)(2,1)}) %all-gather.4.cloned.1.call-update) | async-done | bytes 1048592 | tf_op jit(solution)/shard_map/all_gather | solution.py:16
  71.9 1.9 fusion.17
  73.8 0.7 copy.76
  74.5 0.2 copy.98
  74.7 3.3 convolution_convert_fusion.1
  78.1 0.7 copy-done.10
  78.7 0.1 copy.78
  78.8 0.1 eq.31
  78.9 0.1 eq.27
  79.1 0.1 reshape.259
  79.3 0.9 reduce-window.16
  80.2 0.2 slice_reduce_fusion
  80.4 0.1 fusion.39
  80.6 2.9 scatter_custom_fusion.1
  83.5 2.1 scatter_custom_fusion
  85.7 0.1 broadcast_in_dim.75
  85.8 66.6 %reduce-scatter.2.cloned.1.call-done = bf16[64,2048]{1,0:T(8,128)(2,1)} async-done(((bf16[1024,2048]{1,0:T(8,128)(2,1)}), bf16[64,2048]{1,0:T(8,128)(2,1)}) %reduce-scatter.2.cloned.1.call-update) | async-done | bytes 262160 | tf_op jit(solution)/shard_map/reduce_scatter | solution.py:105
  152.5 1.1 fusion.24
  153.6 1.1 fusion.26
  154.7 3.3 gather_fusion
  158.0 1.8 copy_select_fusion
  159.8 29.3 %all_to_all.20 = bf16[4,16,8,2048]{3,2,0,1:T(8,128)(2,1)S(1)} all-to-all(bf16[4,16,8,2048]{3,2,0,1:T(8,128)(2,1)S(1)} %copy_select_fusion), channel_id=1, replica_groups=mesh['seq'=16,'exp'=16] {'seq'}, dimensions={1} | all-to-all | bytes 4194304 | tf_op jit(solution)/shard_map/all_to_all | solution.py:137
  189.2 0.2 copy.84
  189.4 1.1 broadcast_in_dim.79
  190.5 198.7 %all_to_all.21 = bf16[16,16,8,2048]{3,2,1,0:T(8,128)(2,1)S(1)} all-to-all(bf16[16,16,8,2048]{3,2,1,0:T(8,128)(2,1)S(1)} %bitcast.116), channel_id=1, replica_groups=mesh['seq'=16,'exp'=16] {'exp'}, dimensions={0} | all-to-all | bytes 16777216 | tf_op jit(solution)/shard_map/all_to_all | solution.py:139
  389.2 3.2 fusion.12
  392.5 3.5 fusion.2
  396.0 6.8 convolution_convert_fusion
  402.8 8.3 %copy.85 = bf16[16,16,8,2048]{3,2,0,1:T(8,128)(2,1)} copy(bf16[16,16,8,2048]{3,2,1,0:T(8,128)(2,1)} %bitcast.120) | data formatting | bytes 16777216 | tf_op jit(solution)/shard_map/reshape | solution.py:150
  411.1 100.0 %all_to_all.22 = bf16[16,16,8,2048]{3,2,0,1:T(8,128)(2,1)} all-to-all(bf16[16,16,8,2048]{3,2,0,1:T(8,128)(2,1)} %copy.85), channel_id=1, replica_groups=mesh['seq'=16,'exp'=16] {'seq'}, dimensions={1} | all-to-all | bytes 16777216 | tf_op jit(solution)/shard_map/all_to_all | solution.py:152
  511.1 8.3 %copy.86 = bf16[16,16,8,2048]{3,2,1,0:T(8,128)(2,1)} copy(bf16[16,16,8,2048]{3,2,0,1:T(8,128)(2,1)} %all_to_all.22) | data formatting | bytes 16777216 | tf_op jit(solution)/shard_map/all_to_all | solution.py:152
  519.4 4.8 all-to-all-start.3
  524.2 0.1 copy.89
  524.3 182.6 %all-to-all-done.3 = bf16[16,16,8,2048]{3,2,1,0:T(8,128)(2,1)} async-done(((bf16[16,16,8,2048]{3,2,1,0:T(8,128)(2,1)}), bf16[16,16,8,2048]{3,2,1,0:T(8,128)(2,1)}, u32[]{:S(2)}, u32[]{:S(2)}) %all-to-all-start.3) | async-done | bytes 8388640 | tf_op jit(solution)/shard_map/all_to_all | solution.py:151
  706.9 7.8 %convert_reduce_fusion = f32[4,16,8,2048]{3,2,1,0:T(8,128)} fusion(bf16[16,16,8,2048]{3,2,1,0:T(8,128)(2,1)} %all-to-all-done.3), kind=kLoop, calls=%fused_computation.11 | loop fusion | flops 7340032 | bytes 12582912 | tf_op jit(solution)/shard_map/reduce_sum | solution.py:158
  714.7 7.3 gather_fusion.1
  722.0 4.7 gather.13
  726.7 3.8 multiply_reduce_fusion
  730.5 0.8 fusion.27
  (69 shorter events, 0.9 us)
Async XLA Ops:
  6.5 389.5 %copy-start = (bf16[1,352,2048]{2,1,0:T(8,128)(2,1)S(1)}, bf16[1,352,2048]{2,1,0:T(8,128)(2,1)}, u32[]{:S(2)}) copy-start(bf16[1,352,2048]{2,1,0:T(8,128)(2,1)} %param.33) | copy-start | bytes 4325380
  6.5 9.8 %copy-start.8 = (f32[4,1024]{1,0:T(4,128)S(1)}, f32[4,1024]{1,0:T(4,128)}, u32[]{:S(2)}) copy-start(f32[4,1024]{1,0:T(4,128)} %param.23) | copy-start | bytes 49156
  6.5 65.3 %all-gather.4.cloned.1.call-start = ((), (), s32[]{:S(2)}) async-start(), calls=%async_computation.6 | async-start | bytes 1114112 | tf_op jit(solution)/shard_map/all_gather | solution.py:16
  13.0 0.8 copy-start.6
  15.8 5.9 copy-start.16
  16.5 43.9 %copy-start.4 = (bf16[1024,128]{1,0:T(8,128)(2,1)S(1)}, bf16[1024,128]{1,0:T(8,128)(2,1)}, u32[]{:S(2)}) copy-start(bf16[1024,128]{1,0:T(8,128)(2,1)} %param.22) | copy-start | bytes 786436
  16.5 43.9 %copy-start.5 = (bf16[1024,128]{1,0:T(8,128)(2,1)S(1)}, bf16[1024,128]{1,0:T(8,128)(2,1)}, u32[]{:S(2)}) copy-start(bf16[1024,128]{1,0:T(8,128)(2,1)} %param.21) | copy-start | bytes 786436
  21.6 130.9 %reduce-scatter.2.cloned.1.call-start = ((), (), s32[]{:S(2)}) async-start(), calls=%async_computation.5 | async-start | bytes 4456448 | tf_op jit(solution)/shard_map/reduce_scatter | solution.py:105
  60.7 11.2 %copy-start.12 = (f32[4]{0:T(128)S(1)}, f32[4]{0:T(128)}, u32[]{:S(2)}) copy-start(f32[4]{0:T(128)} %param.25) | copy-start | bytes 52
  71.9 2.8 copy-start.7
  71.9 2.8 copy-start.15
  78.0 0.7 copy-start.10
  78.0 74.4 %copy-start.2 = (bf16[64,2048]{1,0:T(8,128)(2,1)S(1)}, bf16[64,2048]{1,0:T(8,128)(2,1)}, u32[]{:S(2)}) copy-start(bf16[64,2048]{1,0:T(8,128)(2,1)} %param.27) | copy-start | bytes 786436
  78.0 75.6 %copy-start.9 = (f32[2048]{0:T(1024)S(1)}, f32[2048]{0:T(1024)}, u32[]{:S(2)}) copy-start(f32[2048]{0:T(1024)} %param.28) | copy-start | bytes 24580
  190.5 198.7 %copy-start.13 = (bf16[1,352,2048]{2,1,0:T(8,128)(2,1)S(1)}, bf16[1,352,2048]{2,1,0:T(8,128)(2,1)}, u32[]{:S(2)}) copy-start(bf16[1,352,2048]{2,1,0:T(8,128)(2,1)} %param.31) | copy-start | bytes 4325380
  389.2 3.2 copy-start.14
  519.4 4.8 copy-start.11
  519.4 187.5 %all-to-all-start.3 = ((bf16[16,16,8,2048]{3,2,1,0:T(8,128)(2,1)}), bf16[16,16,8,2048]{3,2,1,0:T(8,128)(2,1)}, u32[]{:S(2)}, u32[]{:S(2)}) async-start(bf16[16,16,8,2048]{3,2,1,0:T(8,128)(2,1)} %copy.86), calls=%async_computation.4 | async-start | bytes 16777216 | tf_op jit(solution)/shard_map/all_to_all | solution.py:151
  722.0 9.3 %copy-start.1 = (bf16[1,352,2048]{2,1,0:T(8,128)(2,1)S(1)}, bf16[1,352,2048]{2,1,0:T(8,128)(2,1)}, u32[]{:S(2)}) copy-start(bf16[1,352,2048]{2,1,0:T(8,128)(2,1)} %param.33) | copy-start | bytes 4325380
  726.7 3.8 copy-start.3
Sparse Core Ops, SparseCore 0:
  21.7 50.0 all-gather.3
  78.2 74.2 reduce-scatter.1
where the time goes:
time: 740 us; the launch traced here: 738 us
  blocking collectives  362 us (49%)
  waiting for transfers between devices  259 us (35%)
  local copies, waits for them, and re-layouts  48.7 us (7%)
  other arithmetic  26.9 us (4%)
  matrix products  21.7 us (3%)
  between operations  14.5 us (2%)
    all_to_all x1, blocking collectives, shards(): lax.all_to_all(copies, 'exp', split_axis=0, concat_axis=0, tiled=True)  199 us
    all_to_all x1, waiting for transfers between devices, shards(): lax.all_to_all(lax.all_to_all(piece_out, 'seq', split_axis=1, concat_axis...  183 us
    all_to_all x1, blocking collectives, shards(): lax.all_to_all(piece_out, 'seq', split_axis=1, concat_axis=1, tiled=True)  100 us
    reduce_scatter x1, waiting for transfers between devices, shards(): lax.psum_scatter(jnp.dot(gated_out, out_weight, preferred_element_type=jn...  66.6 us
    unnamed x1, blocking collectives  34.3 us
    all_to_all x1, blocking collectives, shards(): lax.all_to_all(outgoing, 'seq', split_axis=1, concat_axis=1, tiled=True)  29.3 us
  transfers between devices with their start and end apart: 3, of which 3 were waited for; matrix products, arithmetic and copies ran while one was open for 2% of the time, Pallas kernels for 0%

commit v1 on v0

--- a/solution.py
+++ b/solution.py
@@ -149,7 +149,12 @@
     )
     piece_out = piece_out.reshape(block.shape)
     returned = lax.all_to_all(
-        lax.all_to_all(piece_out, "seq", split_axis=1, concat_axis=1, tiled=True),
+        jnp.concatenate(
+            lax.all_to_all(
+                jnp.stack(jnp.split(piece_out, lax.axis_size("seq"), axis=1)), "seq", 0, 0
+            ),
+            axis=1,
+        ),
         "exp",
         split_axis=0,
         concat_axis=0,

time: 740 us -> 731 us (0.988)
  local copies, waits for them, and re-layouts: 48.7 us -> 40.3 us
    all_to_all x1 -> x0, local copies, waits for them, and re-layouts: 8.26 us -> none  [shards(): lax.all_to_all(piece_out, 'seq', split_axis=1, concat_axis=1, tiled=True)]
where the time goes in v1:
time: 731 us; the launch traced here: 729 us
  blocking collectives  361 us (49%)
  waiting for transfers between devices  259 us (35%)
  local copies, waits for them, and re-layouts  40.3 us (6%)
  other arithmetic  27.6 us (4%)
  matrix products  22 us (3%)
  between operations  14.6 us (2%)
    all_to_all x1, blocking collectives, shards(): lax.all_to_all(copies, 'exp', split_axis=0, concat_axis=0, tiled=True)  199 us
    all_to_all x1, waiting for transfers between devices, shards(): lax.all_to_all(jnp.concatenate(lax.all_to_all(jnp.stack(jnp.split(piece_o...  183 us
    all_to_all x1, blocking collectives, shards(): lax.all_to_all(jnp.stack(jnp.split(piece_out, lax.axis_size('seq'), axis=...  98.7 us
    reduce_scatter x1, waiting for transfers between devices, shards(): lax.psum_scatter(jnp.dot(gated_out, out_weight, preferred_element_type=jn...  67.3 us
    unnamed x1, blocking collectives  34.3 us
    all_to_all x1, blocking collectives, shards(): lax.all_to_all(outgoing, 'seq', split_axis=1, concat_axis=1, tiled=True)  29.3 us
  transfers between devices with their start and end apart: 3, of which 3 were waited for; matrix products, arithmetic and copies ran while one was open for 2% of the time, Pallas kernels for 0%

profile of v1, /device:TPU:1, one launch (start us, length us, event | category | flops | bytes accessed | tf_op | source)
XLA Modules:
  0.0 729.3 jit_solution(2057017843514948010)
XLA Ops:
  6.6 0.9 reshape.260
  7.5 4.8 reduce-window.14
  12.4 0.1 copy.112
  12.5 0.1 copy.113
  12.6 0.1 broadcast_add_fusion
  12.8 0.3 copy.114
  13.1 0.8 copy-done.5
  13.8 2.0 reshape.317
  15.9 0.5 copy.119
  16.4 0.8 fusion.58
  17.2 1.2 fusion.29
  18.5 3.1 while.26
  18.5 0.7 bitcast_dynamic-update-slice_fusion.2
  19.2 0.1 bitcast_add_fusion.2
  19.3 0.7 bitcast_dynamic-update-slice_fusion.2
  19.9 0.1 bitcast_add_fusion.2
  20.1 0.7 bitcast_dynamic-update-slice_fusion.2
  20.8 0.7 bitcast_dynamic-update-slice_fusion.2
  21.6 0.6 convert_element_type.96
  22.4 0.6 dynamic-slice
  23.6 0.2 dynamic-update-slice
  23.9 34.3 %all-reduce = bf16[64]{0:T(256)(128)(2,1)S(1)} all-reduce(bf16[64]{0:T(256)(128)(2,1)S(1)} %dynamic-update-slice), channel_id=2, replica_groups=mesh['seq'=16,'exp'=16] {'seq'}, use_global_device_ids=true, to_apply=%add | all-reduce | flops 64 | bytes 256
  58.2 0.1 reshape.307
  58.3 2.0 copy.124
  60.4 0.7 subtract_exponential_fusion
  61.0 1.2 fusion.74
  62.3 1.4 fusion.14
  63.7 8.8 %all-gather.4.cloned.1.call-done = bf16[64,64,128]{2,1,0:T(8,128)(2,1)} async-done(((bf16[4,64,128]{2,1,0:T(8,128)(2,1)}), bf16[64,64,128]{2,1,0:T(8,128)(2,1)}) %all-gather.4.cloned.1.call-update) | async-done | bytes 1048592 | tf_op jit(solution)/shard_map/all_gather | solution.py:16
  72.6 1.8 fusion.17
  74.3 0.7 copy.123
  75.0 0.2 copy.176
  75.3 4.7 convolution_convert_fusion.1
  80.0 0.1 copy.125
  80.1 0.1 eq.31
  80.3 0.1 eq.27
  80.4 0.1 reshape.265
  80.6 0.9 reduce-window.16
  81.5 0.2 slice_reduce_fusion
  81.8 0.1 fusion.55
  81.9 2.9 scatter_custom_fusion.1
  84.8 2.1 scatter_custom_fusion
  87.0 0.1 broadcast_in_dim.75
  87.1 67.3 %reduce-scatter.2.cloned.1.call-done = bf16[64,2048]{1,0:T(8,128)(2,1)} async-done(((bf16[1024,2048]{1,0:T(8,128)(2,1)}), bf16[64,2048]{1,0:T(8,128)(2,1)}) %reduce-scatter.2.cloned.1.call-update) | async-done | bytes 262160 | tf_op jit(solution)/shard_map/reduce_scatter | solution.py:105
  154.5 1.1 fusion.24
  155.6 1.1 fusion.26
  156.7 3.3 gather_fusion
  160.0 1.8 copy_select_fusion
  161.8 29.3 %all_to_all.20 = bf16[4,16,8,2048]{3,2,0,1:T(8,128)(2,1)S(1)} all-to-all(bf16[4,16,8,2048]{3,2,0,1:T(8,128)(2,1)S(1)} %copy_select_fusion), channel_id=1, replica_groups=mesh['seq'=16,'exp'=16] {'seq'}, dimensions={1} | all-to-all | bytes 4194304 | tf_op jit(solution)/shard_map/all_to_all | solution.py:137
  191.2 0.2 copy.131
  191.4 1.1 broadcast_in_dim.79
  192.5 198.7 %all_to_all.21 = bf16[16,16,8,2048]{3,2,1,0:T(8,128)(2,1)S(1)} all-to-all(bf16[16,16,8,2048]{3,2,1,0:T(8,128)(2,1)S(1)} %bitcast.215), channel_id=1, replica_groups=mesh['seq'=16,'exp'=16] {'exp'}, dimensions={0} | all-to-all | bytes 16777216 | tf_op jit(solution)/shard_map/all_to_all | solution.py:139
  391.2 3.2 fusion.12
  394.5 3.6 fusion.2
  398.1 4.8 convolution_convert_fusion
  403.6 98.7 %all_to_all.22 = bf16[16,16,1,8,2048]{4,3,1,2,0:T(8,128)(2,1)} all-to-all(bf16[16,16,1,8,2048]{4,3,1,2,0:T(8,128)(2,1)S(1)} %fusion.31), channel_id=1, replica_groups=mesh['seq'=16,'exp'=16] {'seq'}, dimensions={0} | all-to-all | bytes 16777216 | tf_op jit(solution)/shard_map/all_to_all | solution.py:153
  502.3 8.3 %copy.148 = bf16[16,16,8,2048]{3,2,1,0:T(8,128)(2,1)} copy(bf16[16,16,8,2048]{3,2,0,1:T(8,128)(2,1)} %bitcast.216) | data formatting | bytes 16777216 | tf_op jit(solution)/shard_map/reshape | solution.py:152
  510.6 4.8 all-to-all-start.3
  515.4 0.1 copy.151
  515.5 182.6 %all-to-all-done.3 = bf16[16,16,8,2048]{3,2,1,0:T(8,128)(2,1)} async-done(((bf16[16,16,8,2048]{3,2,1,0:T(8,128)(2,1)}), bf16[16,16,8,2048]{3,2,1,0:T(8,128)(2,1)}, u32[]{:S(2)}, u32[]{:S(2)}) %all-to-all-start.3) | async-done | bytes 8388640 | tf_op jit(solution)/shard_map/all_to_all | solution.py:151
  698.1 7.8 %convert_reduce_fusion = f32[4,16,8,2048]{3,2,1,0:T(8,128)} fusion(bf16[16,16,8,2048]{3,2,1,0:T(8,128)(2,1)} %all-to-all-done.3), kind=kLoop, calls=%fused_computation.11 | loop fusion | flops 7340032 | bytes 12582912 | tf_op jit(solution)/shard_map/reduce_sum | solution.py:163
  705.9 7.4 %gather_fusion.1 = f32[384,2048]{1,0:T(8,128)} fusion(f32[512,2048]{1,0:T(8,128)} %bitcast.214, s32[1024]{0:T(1024)S(1)} %pad_clamp_fusion), kind=kCustom, calls=%fused_computation.1 | custom fusion | bytes 6292992 | tf_op jit(solution)/shard_map/gather | solution.py:166
  713.3 4.6 gather.13
  717.9 3.7 multiply_reduce_fusion
  721.7 0.8 fusion.27
  (78 shorter events, 1.3 us)
Async XLA Ops:
  6.5 391.5 %copy-start = (bf16[1,352,2048]{2,1,0:T(8,128)(2,1)S(1)}, bf16[1,352,2048]{2,1,0:T(8,128)(2,1)}, u32[]{:S(2)}) copy-start(bf16[1,352,2048]{2,1,0:T(8,128)(2,1)} %param.33) | copy-start | bytes 4325380
  6.5 15.9 %copy-start.13 = (u32[256]{0:T(256)S(1)}, u32[256]{0:T(256)}, u32[]{:S(2)}) copy-start(u32[256]{0:T(256)} %constant.118) | copy-start | bytes 3076
  6.5 15.8 %copy-start.6 = (f32[4,1024]{1,0:T(4,128)S(1)}, f32[4,1024]{1,0:T(4,128)}, u32[]{:S(2)}) copy-start(f32[4,1024]{1,0:T(4,128)} %param.23) | copy-start | bytes 49156
  6.5 54.5 %copy-start.4 = (bf16[1024,128]{1,0:T(8,128)(2,1)S(1)}, bf16[1024,128]{1,0:T(8,128)(2,1)}, u32[]{:S(2)}) copy-start(bf16[1024,128]{1,0:T(8,128)(2,1)} %param.22) | copy-start | bytes 786436
  6.5 66.0 %all-gather.4.cloned.1.call-start = ((), (), s32[]{:S(2)}) async-start(), calls=%async_computation.6 | async-start | bytes 1114112 | tf_op jit(solution)/shard_map/all_gather | solution.py:16
  13.0 0.8 copy-start.5
  18.5 54.1 %copy-start.10 = (f32[4]{0:T(128)S(1)}, f32[4]{0:T(128)}, u32[]{:S(2)}) copy-start(f32[4]{0:T(128)} %param.25) | copy-start | bytes 52
  22.3 132.2 %reduce-scatter.2.cloned.1.call-start = ((), (), s32[]{:S(2)}) async-start(), calls=%async_computation.5 | async-start | bytes 4456448 | tf_op jit(solution)/shard_map/reduce_scatter | solution.py:105
  75.2 4.8 copy-start.8
  75.3 79.2 %copy-start.2 = (bf16[64,2048]{1,0:T(8,128)(2,1)S(1)}, bf16[64,2048]{1,0:T(8,128)(2,1)}, u32[]{:S(2)}) copy-start(bf16[64,2048]{1,0:T(8,128)(2,1)} %param.27) | copy-start | bytes 786436
  75.3 80.3 %copy-start.7 = (f32[2048]{0:T(1024)S(1)}, f32[2048]{0:T(1024)}, u32[]{:S(2)}) copy-start(f32[2048]{0:T(1024)} %param.28) | copy-start | bytes 24580
  192.5 198.7 %copy-start.11 = (bf16[1,352,2048]{2,1,0:T(8,128)(2,1)S(1)}, bf16[1,352,2048]{2,1,0:T(8,128)(2,1)}, u32[]{:S(2)}) copy-start(bf16[1,352,2048]{2,1,0:T(8,128)(2,1)} %param.31) | copy-start | bytes 4325380
  391.2 3.2 copy-start.12
  510.6 4.8 copy-start.9
  510.6 187.5 %all-to-all-start.3 = ((bf16[16,16,8,2048]{3,2,1,0:T(8,128)(2,1)}), bf16[16,16,8,2048]{3,2,1,0:T(8,128)(2,1)}, u32[]{:S(2)}, u32[]{:S(2)}) async-start(bf16[16,16,8,2048]{3,2,1,0:T(8,128)(2,1)} %copy.148), calls=%async_computation.4 | async-start | bytes 16777216 | tf_op jit(solution)/shard_map/all_to_all | solution.py:151
  705.9 16.6 %copy-start.1 = (bf16[1,352,2048]{2,1,0:T(8,128)(2,1)S(1)}, bf16[1,352,2048]{2,1,0:T(8,128)(2,1)}, u32[]{:S(2)}) copy-start(bf16[1,352,2048]{2,1,0:T(8,128)(2,1)} %param.33) | copy-start | bytes 4325380
  713.3 8.4 %copy-start.3 = (bf16[64,2048]{1,0:T(8,128)(2,1)S(1)}, bf16[64,2048]{1,0:T(8,128)(2,1)}, u32[]{:S(2)}) copy-start(bf16[64,2048]{1,0:T(8,128)(2,1)} %reduce-scatter.2.cloned.1.call-done) | copy-start | bytes 786436
Sparse Core Ops, SparseCore 0:
  22.4 50.0 all-gather.3
  80.1 74.2 reduce-scatter.1
